TPU v7x, 512 devices: a whole 4x8x8 slice. The times are simulated.
512 devices in a mesh: sub: 128 (over z_hi, x, y, core), scen: 4 (over z_lo).
Axes of the slice: x: 4, y: 8, z: 8 (z_hi: 2, z_lo: 4; z = z_hi * 4 + z_lo), core: 2. Of those that a mesh axis runs over, the one named last changes fastest.
Arguments:
- inverse_matrix: bfloat16 [128, 1024, 1024], P('sub'), may hold values from -1 to 1
- objective_grad: bfloat16 [48, 128, 64, 1024], P(None, 'sub', 'scen'), may hold values from -6 to 6
- final_adjoint: float32 [128, 64, 1024], P('sub', 'scen'), may hold values from -6 to 6
- companion: float32 [128, 1024], P('sub'), may hold values from 0.95 to 0.995
- port_node: int32 [128, 4, 8], P('sub'), may hold values from 0 to 1023
- line_count: int32 [128, 4], P('sub'), may hold values from 1 to 8, as said below
- line_delay: int32 [128, 4, 8], P('sub'), may hold values from 24 to 47, as said below
- line_admittance: float32 [128, 4, 8], P('sub'), may hold values from 0.3 to 1.2
- later_history: float32 [128, 4, 8, 48, 64], P('sub', None, None, None, 'scen'), may hold values from -6 to 6
- conv_node: int32 [128, 16], P('sub'), may hold values from 0 to 1023
- conv_drive: float32 [128, 48, 64, 16], P('sub', None, 'scen'), may hold values from -0.25 to 0.25
- fault_bus: int32 [64], P('scen'), may hold values from 0 to 131071
- fault_current: float32 [48, 64], P(None, 'scen'), may hold values from -12 to 12
- fault_voltage: float32 [48, 64], P(None, 'scen'), may hold values from -2 to 2
Outputs:
- adjoint_start: float32 [128, 64, 1024], P('sub', 'scen')
- earlier_history: float32 [128, 4, 8, 48, 64], P('sub', None, None, None, 'scen')
- control_sens: float32 [128, 16], P('sub')
- fault_sens: float32 [64], P('scen')
Inputs may be any that keep to these rules, and one draw needn't show every extreme that they name: line_count[p, e] equals line_count of the partner subnetwork in the opposite direction; the most is reached in every draw. `line_delay`: both ends of a line have the same delay; both ends of the range are reached in every draw.
All inputs are finite; a program needn't handle non-finite values.
Results may differ from a plain program's by a relative error of at most 0.0088.
Values sent between devices are 32-bit elements; how exact they have to be, the bound alone decides.
No kernel may reach another device: no remote copies, remote signals or barrier semaphores. Data moves between devices by JAX's collectives and lax.ppermute only.
A program may use at most 64 MiB of HBM per device.

v0:
```python
import jax
import jax.numpy as jnp
import numpy as np
from jax.sharding import Mesh
from jax import lax
from jax.sharding import PartitionSpec as P

PRECISE = lax.Precision.HIGHEST
SUB = ("z_hi", "x", "y", "core")
SUB_SIZES = (2, 4, 8, 2)


def sum_over_sub(value):
    for axis in reversed(SUB):
        value = lax.psum(value, axis)
    return value


def passed_along(value, axis, steps):
    count = lax.axis_size(axis)
    pairs = [(source, (source + steps) % count) for source in range(count)]
    return lax.ppermute(value, axis, pairs)


def body(
    inverse_matrix,
    objective_grad,
    final_adjoint,
    companion,
    port_node,
    line_count,
    line_delay,
    line_admittance,
    later_history,
    conv_node,
    conv_drive,
    fault_bus,
    fault_current,
    fault_voltage,
):
    node_count = inverse_matrix.shape[1]
    scen_rows = objective_grad.shape[2]
    slot_count = port_node.shape[2]
    port_total = 4 * slot_count
    conv_count = conv_node.shape[1]
    block_len = later_history.shape[3] // 2
    blocks = objective_grad.shape[0] // block_len
    sub_count = lax.axis_size(SUB)
    grid_width = max(2, sub_count // 16)
    offsets = (1, -1, grid_width, -grid_width)
    opposite = (1, 0, 3, 2)
    sub_index = lax.axis_index(SUB)
    weights = inverse_matrix[0]
    live_mask = (lax.iota(jnp.int32, slot_count)[None, :] < line_count[0][:, None]).astype(
        jnp.float32
    )
    node_iota = lax.iota(jnp.int32, node_count)
    pick_table = jnp.concatenate(
        [
            node_iota[:, None] == port_node[0].reshape(port_total)[None, :],
            node_iota[:, None] == conv_node[0][None, :],
        ],
        axis=1,
    ).astype(jnp.float32)
    spread_table = jnp.transpose(pick_table[:, :port_total])
    line_scale = (line_admittance[0] * live_mask).reshape(port_total)
    fault_table = (node_iota[None, :] == (fault_bus - sub_index * node_count)[:, None]).astype(
        jnp.float32
    )
    window = later_history[0]
    adjoint_next = final_adjoint[0]
    control_local = jnp.zeros((conv_count,), jnp.float32)
    fault_local = jnp.zeros((scen_rows,), jnp.float32)
    block_rows = lax.iota(jnp.int32, block_len)
    time_iota = lax.iota(jnp.int32, 2 * block_len)

    def one_step(adjoint_prev, inputs):
        grad_now, inflow_now, current_now = inputs
        right_side = (
            grad_now.astype(jnp.float32)
            + companion[0][None, :] * adjoint_prev
            + inflow_now
            + current_now[:, None] * fault_table
        )
        adjoint = jnp.dot(
            right_side.astype(jnp.bfloat16), weights, preferred_element_type=jnp.float32
        )
        return (adjoint, adjoint)

    for block_id in reversed(range(blocks)):
        block_start = block_id * block_len
        target = block_rows[None, None, :] + line_delay[0][:, :, None] - block_len
        time_table = (target[..., None] == time_iota).astype(jnp.float32)
        picked = (
            jnp.einsum("ecji,ecis->jsec", time_table, window, precision=PRECISE).reshape(
                block_len * scen_rows, port_total
            )
            * line_scale[None, :]
        )
        inflow = jnp.dot(picked, spread_table, precision=PRECISE).reshape(
            block_len, scen_rows, node_count
        )
        adjoint_next, adjoint_block = lax.scan(
            one_step,
            adjoint_next,
            (
                objective_grad[block_start : block_start + block_len, 0],
                inflow,
                fault_current[block_start : block_start + block_len],
            ),
            reverse=True,
        )
        samples = jnp.dot(
            adjoint_block.reshape(block_len * scen_rows, node_count), pick_table, precision=PRECISE
        )
        series = (
            jnp.transpose(
                samples[:, :port_total].reshape(block_len, scen_rows, 4, slot_count), (2, 3, 0, 1)
            )
            * live_mask[:, :, None, None]
        )
        outbound = series.reshape(4, slot_count, block_len * scen_rows)
        control_term = jnp.sum(
            samples[:, port_total:].reshape(block_len, scen_rows, conv_count)
            * conv_drive[0, block_start : block_start + block_len],
            axis=(0, 1),
        )
        fault_term = jnp.sum(
            jnp.sum(adjoint_block * fault_table[None], axis=2)
            * fault_voltage[block_start : block_start + block_len],
            axis=0,
        )
        control_local = control_local + lax.psum(control_term, "scen")
        fault_local = fault_local + fault_term
        received = jnp.stack(
            [
                passed_along(outbound[opposite[direction]], SUB, -offsets[direction])
                for direction in range(4)
            ]
        )
        window = jnp.concatenate(
            [received.reshape(4, slot_count, block_len, scen_rows), window[:, :, :block_len]],
            axis=2,
        )
    fault_local = sum_over_sub(fault_local)
    return (adjoint_next[None], window[None], control_local[None], fault_local)


def solution(mesh):
    sub_mesh = Mesh(
        np.asarray(mesh.devices).reshape(SUB_SIZES + (mesh.shape["scen"],)), SUB + ("scen",)
    )
    return jax.shard_map(
        body,
        mesh=sub_mesh,
        in_specs=(
            P(SUB, None, None),
            P(None, SUB, "scen", None),
            P(SUB, "scen", None),
            P(SUB, None),
            P(SUB, None, None),
            P(SUB, None),
            P(SUB, None, None),
            P(SUB, None, None),
            P(SUB, None, None, None, "scen"),
            P(SUB, None),
            P(SUB, None, "scen", None),
            P("scen"),
            P(None, "scen"),
            P(None, "scen"),
        ),
        out_specs=(P(SUB, "scen", None), P(SUB, None, None, None, "scen"), P(SUB, None), P("scen")),
        check_vma=False,
    )
```

profile of v0, /device:TPU:4, one launch (start us, length us, event | category | flops | bytes accessed | tf_op | source)
XLA Modules:
  0.0 258.3 jit_solution(13217957040212197619)
XLA Ops:
  6.0 2.5 slice_bitcast_fusion
  9.3 2.0 fusion.45
  12.7 45.9 %while.34 = (s32[]{:T(128)}, f32[16,1024]{1,0:T(8,128)S(1)}, f32[24,16,1024]{2,1,0:T(8,128)}, bf16[24,16,1024]{2,1,0:T(8,128)(2,1)}, f32[1,1024]{1,0:T(1,128)S(1...) while((s32[]{:T(128)}, f32[16,1024]{1,0:T(8,128)S(1)}, ...), condition=%wide.region_1.2_spmd.clone, body=%wide.region_0.1_spmd.clone.sunk | while | flops 33685504 | bytes 2528637 | solution.py:103
  12.7 1.9 bitcast_dynamic-update-slice_fusion.4
  20.4 1.9 bitcast_dynamic-update-slice_fusion.4
  24.2 1.9 bitcast_dynamic-update-slice_fusion.4
  29.9 1.9 bitcast_dynamic-update-slice_fusion.4
  41.4 1.9 bitcast_dynamic-update-slice_fusion.4
  45.2 1.9 bitcast_dynamic-update-slice_fusion.4
  51.0 1.9 bitcast_dynamic-update-slice_fusion.4
  52.9 1.9 bitcast_dynamic-update-slice_fusion.4
  54.8 1.9 bitcast_dynamic-update-slice_fusion.4
  56.7 1.9 bitcast_dynamic-update-slice_fusion.4
  58.7 2.3 fusion.57
  63.4 4.8 %collective-permute-start = (f32[8,384]{1,0:T(8,128)}, f32[8,384]{1,0:T(8,128)S(1)}, u32[]{:S(2)}, u32[]{:S(2)}) collective-permute-start(f32[8,384]{1,0:T(8,128)} %squeeze.91), channel_id=1, source_target_pairs={{0,508},{4,0},{8,4},{12,8},{16,12},{20,16},{24,20},{28,24},{32,28}... | collective-permute-start | bytes 36872 | tf_op jit(solution)/shard_map/ppermute | solution.py:22
  68.2 1.9 collective-permute-start.1
  70.8 5.3 %collective-permute-start.2 = (f32[8,384]{1,0:T(8,128)}, f32[8,384]{1,0:T(8,128)}, u32[]{:S(2)}, u32[]{:S(2)}) collective-permute-start(f32[8,384]{1,0:T(8,128)} %squeeze.93), channel_id=1, source_target_pairs={{0,480},{4,484},{8,488},{12,492},{16,496},{20,500},{24,504},{28,50... | collective-permute-start | bytes 36872 | tf_op jit(solution)/shard_map/ppermute | solution.py:22
  76.3 4.4 %collective-permute-start.3 = (f32[8,384]{1,0:T(8,128)S(1)}, f32[8,384]{1,0:T(8,128)}, u32[]{:S(2)}, u32[]{:S(2)}) collective-permute-start(f32[8,384]{1,0:T(8,128)S(1)} %squeeze.94), channel_id=1, source_target_pairs={{0,32},{4,36},{8,40},{12,44},{16,48},{20,52},{24,56},{28,60},{32,6... | collective-permute-start | bytes 36872 | tf_op jit(solution)/shard_map/ppermute | solution.py:22
  90.7 2.0 fusion.43
  94.1 62.0 %while.35 = (s32[]{:T(128)}, f32[16,1024]{1,0:T(8,128)S(1)}, f32[24,16,1024]{2,1,0:T(8,128)}, bf16[24,16,1024]{2,1,0:T(8,128)(2,1)S(1)}, f32[1,1024]{1,0:T(1,128...) while((s32[]{:T(128)}, f32[16,1024]{1,0:T(8,128)S(1)}, ...), condition=%wide.region_3.4_spmd.clone, body=%wide.region_2.3_spmd.clone.sunk | while | flops 33685504 | bytes 2529533 | solution.py:103
  125.8 1.9 bitcast_dynamic-update-slice_fusion.5
  141.3 1.9 bitcast_dynamic-update-slice_fusion.5
  156.1 2.3 multiply_reduce_fusion
  159.9 6.1 %collective-permute-start.4 = (f32[8,384]{1,0:T(8,128)S(1)}, f32[8,384]{1,0:T(8,128)S(1)}, u32[]{:S(2)}, u32[]{:S(2)}) collective-permute-start(f32[8,384]{1,0:T(8,128)S(1)} %squeeze.95), channel_id=1, source_target_pairs={{0,508},{4,0},{8,4},{12,8},{16,12},{20,16},{24,20},{28,24},{32,28}... | collective-permute-start | bytes 36872 | tf_op jit(solution)/shard_map/ppermute | solution.py:22
  166.1 1.9 collective-permute-start.5
  168.1 3.0 %collective-permute-start.6 = (f32[8,384]{1,0:T(8,128)S(1)}, f32[8,384]{1,0:T(8,128)S(1)}, u32[]{:S(2)}, u32[]{:S(2)}) collective-permute-start(f32[8,384]{1,0:T(8,128)S(1)} %squeeze.97), channel_id=1, source_target_pairs={{0,480},{4,484},{8,488},{12,492},{16,496},{20,500},{24,504},{28,50... | collective-permute-start | bytes 36872 | tf_op jit(solution)/shard_map/ppermute | solution.py:22
  171.3 6.7 %collective-permute-start.7 = (f32[8,384]{1,0:T(8,128)S(1)}, f32[8,384]{1,0:T(8,128)S(1)}, u32[]{:S(2)}, u32[]{:S(2)}) collective-permute-start(f32[8,384]{1,0:T(8,128)S(1)} %squeeze.98), channel_id=1, source_target_pairs={{0,32},{4,36},{8,40},{12,44},{16,48},{20,52},{24,56},{28,60},{32,6... | collective-permute-start | bytes 36872 | tf_op jit(solution)/shard_map/ppermute | solution.py:22
  178.9 2.5 psum.44
  181.4 18.4 %psum.45 = f32[16]{0:T(128)S(1)} all-reduce(f32[16]{0:T(128)S(1)} %psum.44), channel_id=1, replica_groups=mesh['z_hi'=2,'x'=4,'y'=8,'core'=2,'scen'=4] {'y'}, use_global_device_ids=true, to_apply=%region_13.14 | all-reduce | flops 16 | bytes 128 | tf_op jit(solution)/shard_map/psum | solution.py:15
  199.8 32.4 %psum.46 = f32[16]{0:T(128)S(1)} all-reduce(f32[16]{0:T(128)S(1)} %psum.45), channel_id=1, replica_groups=mesh['z_hi'=2,'x'=4,'y'=8,'core'=2,'scen'=4] {'x'}, use_global_device_ids=true, to_apply=%region_14.15 | all-reduce | flops 16 | bytes 128 | tf_op jit(solution)/shard_map/psum | solution.py:15
  232.2 12.4 %psum.47 = f32[16]{0:T(128)} all-reduce(f32[16]{0:T(128)S(1)} %psum.46), channel_id=1, replica_groups=mesh['z_hi'=2,'x'=4,'y'=8,'core'=2,'scen'=4] {'z_hi'}, use_global_device_ids=true, to_apply=%region_15.16 | all-reduce | flops 16 | bytes 128 | tf_op jit(solution)/shard_map/psum | solution.py:15
  244.6 12.1 %psum.48 = f32[16]{0:T(128)} all-reduce(f32[16]{0:T(128)S(1)} %add.151), channel_id=1, replica_groups=mesh['z_hi'=2,'x'=4,'y'=8,'core'=2,'scen'=4] {'scen'}, use_global_device_ids=true, to_apply=%region_5.6 | all-reduce | flops 16 | bytes 128 | tf_op jit(solution)/shard_map/psum | solution.py:133
  (265 shorter events, 111.0 us)
Async XLA Ops:
  3.6 5.7 %copy-start.24 = (s32[32]{0:T(128)}, s32[32]{0:T(128)S(1)}, u32[]{:S(2)}) copy-start(s32[32]{0:T(128)S(1)} %eq.71) | copy-start | bytes 388
  6.0 2.5 copy-start.20
  6.0 3.3 %copy-start.29 = (s32[16]{0:T(128)S(1)}, s32[16]{0:T(128)}, u32[]{:S(2)}) copy-start(s32[16]{0:T(128)} %param.29) | copy-start | bytes 196
  9.2 49.5 %copy-start.11 = (pred[1024,32]{0,1:T(8,128)(4,1)}, pred[1024,32]{0,1:T(8,128)(4,1)S(1)}, u32[]{:S(2)}) copy-start(pred[1024,32]{0,1:T(8,128)(4,1)S(1)} %iota_compare_fusion.5) | copy-start | bytes 98308
  9.3 3.4 %copy-start.26 = (f32[32]{0:T(128)}, f32[32]{0:T(128)S(1)}, u32[]{:S(2)}) copy-start(f32[32]{0:T(128)S(1)} %broadcast_select_fusion) | copy-start | bytes 388
  9.3 3.4 %copy-start = (bf16[1,1024,1024]{2,1,0:T(8,128)(2,1)S(1)}, bf16[1,1024,1024]{2,1,0:T(8,128)(2,1)}, u32[]{:S(2)}) copy-start(bf16[1,1024,1024]{2,1,0:T(8,128)(2,1)} %param.18) | copy-start | bytes 6291460
  9.3 3.4 %copy-start.3 = (f32[1,16,1024]{2,1,0:T(8,128)S(1)}, f32[1,16,1024]{2,1,0:T(8,128)}, u32[]{:S(2)}) copy-start(f32[1,16,1024]{2,1,0:T(8,128)} %param.20) | copy-start | bytes 196612
  9.3 3.4 %copy-start.9 = (f32[1,1024]{1,0:T(1,128)S(1)}, f32[1,1024]{1,0:T(1,128)}, u32[]{:S(2)}) copy-start(f32[1,1024]{1,0:T(1,128)} %param.21) | copy-start | bytes 12292
  12.7 45.9 %copy-start.28 = (s32[1,16]{1,0:T(1,128)S(1)}, s32[1,16]{1,0:T(1,128)}, u32[]{:S(2)}) copy-start(s32[1,16]{1,0:T(1,128)} %param.27) | copy-start | bytes 196
  61.6 19.8 %copy-start.8 = (f32[1,48,16,16]{1,3,2,0:T(8,128)S(1)}, f32[1,48,16,16]{1,3,2,0:T(8,128)}, u32[]{:S(2)}) copy-start(f32[1,48,16,16]{1,3,2,0:T(8,128)} %param.28) | copy-start | bytes 147460
  61.6 20.4 %copy-start.21 = (f32[48,16]{0,1:T(8,128)S(1)}, f32[48,16]{0,1:T(8,128)}, u32[]{:S(2)}) copy-start(f32[48,16]{0,1:T(8,128)} %param.31) | copy-start | bytes 9220
  61.8 20.3 %copy-start.22 = (f32[24,16]{0,1:T(8,128)S(1)}, f32[24,16]{0,1:T(8,128)}, u32[]{:S(2)}) copy-start(f32[24,16]{0,1:T(8,128)} %get-tuple-element.466) | copy-start | bytes 4612
  63.4 23.4 %collective-permute-start = (f32[8,384]{1,0:T(8,128)}, f32[8,384]{1,0:T(8,128)S(1)}, u32[]{:S(2)}, u32[]{:S(2)}) collective-permute-start(f32[8,384]{1,0:T(8,128)} %squeeze.91), channel_id=1, source_target_pairs={{0,508},{4,0},{8,4},{12,8},{16,12},{20,16},{24,20},{28,24},{32,28}... | collective-permute-start | bytes 36872 | tf_op jit(solution)/shard_map/ppermute | solution.py:22
  68.2 18.7 %collective-permute-start.1 = (f32[8,384]{1,0:T(8,128)S(1)}, f32[8,384]{1,0:T(8,128)S(1)}, u32[]{:S(2)}, u32[]{:S(2)}) collective-permute-start(f32[8,384]{1,0:T(8,128)S(1)} %squeeze.92), channel_id=1, source_target_pairs={{0,4},{4,8},{8,12},{12,16},{16,20},{20,24},{24,28},{28,32},{32,36}... | collective-permute-start | bytes 36872 | tf_op jit(solution)/shard_map/ppermute | solution.py:22
  70.8 16.3 %collective-permute-start.2 = (f32[8,384]{1,0:T(8,128)}, f32[8,384]{1,0:T(8,128)}, u32[]{:S(2)}, u32[]{:S(2)}) collective-permute-start(f32[8,384]{1,0:T(8,128)} %squeeze.93), channel_id=1, source_target_pairs={{0,480},{4,484},{8,488},{12,492},{16,496},{20,500},{24,504},{28,50... | collective-permute-start | bytes 36872 | tf_op jit(solution)/shard_map/ppermute | solution.py:22
  76.3 11.8 %collective-permute-start.3 = (f32[8,384]{1,0:T(8,128)S(1)}, f32[8,384]{1,0:T(8,128)}, u32[]{:S(2)}, u32[]{:S(2)}) collective-permute-start(f32[8,384]{1,0:T(8,128)S(1)} %squeeze.94), channel_id=1, source_target_pairs={{0,32},{4,36},{8,40},{12,44},{16,48},{20,52},{24,56},{28,60},{32,6... | collective-permute-start | bytes 36872 | tf_op jit(solution)/shard_map/ppermute | solution.py:22
  85.2 5.5 %copy-start.25 = (s32[32]{0:T(128)S(1)}, s32[32]{0:T(128)}, u32[]{:S(2)}) copy-start(s32[32]{0:T(128)} %copy-done.24) | copy-start | bytes 388
  85.2 5.5 %copy-start.27 = (f32[32]{0:T(128)S(1)}, f32[32]{0:T(128)}, u32[]{:S(2)}) copy-start(f32[32]{0:T(128)} %copy-done.26) | copy-start | bytes 388
  88.1 2.5 copy-start.4
  94.1 62.0 %copy-start.13 = (f32[16,1024]{1,0:T(8,128)S(1)}, f32[16,1024]{1,0:T(8,128)}, u32[]{:S(2)}) copy-start(f32[16,1024]{1,0:T(8,128)} %fusion.55) | copy-start | bytes 196612
  156.1 2.4 copy-start.1
  156.1 2.4 copy-start.12
  159.4 18.6 %copy-start.16 = (f32[384,16]{0,1:T(8,128)S(1)}, f32[384,16]{0,1:T(8,128)}, u32[]{:S(2)}) copy-start(f32[384,16]{0,1:T(8,128)} %squeeze.100) | copy-start | bytes 73732
  159.4 18.6 %copy-start.17 = (f32[384,16]{0,1:T(8,128)S(1)}, f32[384,16]{0,1:T(8,128)}, u32[]{:S(2)}) copy-start(f32[384,16]{0,1:T(8,128)} %squeeze.99) | copy-start | bytes 73732
  159.4 19.4 %copy-start.18 = (f32[24,16]{1,0:T(8,128)S(1)}, f32[24,16]{1,0:T(8,128)}, u32[]{:S(2)}) copy-start(f32[24,16]{1,0:T(8,128)} %copy.62) | copy-start | bytes 4612
  159.4 19.4 %copy-start.19 = (f32[24,16]{1,0:T(8,128)S(1)}, f32[24,16]{1,0:T(8,128)}, u32[]{:S(2)}) copy-start(f32[24,16]{1,0:T(8,128)} %copy.63) | copy-start | bytes 4612
  159.6 97.8 %copy-start.5 = (f32[1,8,24,16]{2,3,1,0:T(8,128)S(1)}, f32[1,8,24,16]{2,3,1,0:T(8,128)}, u32[]{:S(2)}) copy-start(f32[1,8,24,16]{2,3,1,0:T(8,128)} %copy-done.4) | copy-start | bytes 36868
  159.6 97.8 %copy-start.7 = (f32[1,8,24,16]{2,3,1,0:T(8,128)S(1)}, f32[1,8,24,16]{2,3,1,0:T(8,128)}, u32[]{:S(2)}) copy-start(f32[1,8,24,16]{2,3,1,0:T(8,128)} %copy-done.6) | copy-start | bytes 36868
  159.9 96.8 %collective-permute-start.4 = (f32[8,384]{1,0:T(8,128)S(1)}, f32[8,384]{1,0:T(8,128)S(1)}, u32[]{:S(2)}, u32[]{:S(2)}) collective-permute-start(f32[8,384]{1,0:T(8,128)S(1)} %squeeze.95), channel_id=1, source_target_pairs={{0,508},{4,0},{8,4},{12,8},{16,12},{20,16},{24,20},{28,24},{32,28}... | collective-permute-start | bytes 36872 | tf_op jit(solution)/shard_map/ppermute | solution.py:22
  166.1 90.8 %collective-permute-start.5 = (f32[8,384]{1,0:T(8,128)S(1)}, f32[8,384]{1,0:T(8,128)S(1)}, u32[]{:S(2)}, u32[]{:S(2)}) collective-permute-start(f32[8,384]{1,0:T(8,128)S(1)} %squeeze.96), channel_id=1, source_target_pairs={{0,4},{4,8},{8,12},{12,16},{16,20},{20,24},{24,28},{28,32},{32,36}... | collective-permute-start | bytes 36872 | tf_op jit(solution)/shard_map/ppermute | solution.py:22
  168.1 88.9 %collective-permute-start.6 = (f32[8,384]{1,0:T(8,128)S(1)}, f32[8,384]{1,0:T(8,128)S(1)}, u32[]{:S(2)}, u32[]{:S(2)}) collective-permute-start(f32[8,384]{1,0:T(8,128)S(1)} %squeeze.97), channel_id=1, source_target_pairs={{0,480},{4,484},{8,488},{12,492},{16,496},{20,500},{24,504},{28,50... | collective-permute-start | bytes 36872 | tf_op jit(solution)/shard_map/ppermute | solution.py:22
  171.3 86.0 %collective-permute-start.7 = (f32[8,384]{1,0:T(8,128)S(1)}, f32[8,384]{1,0:T(8,128)S(1)}, u32[]{:S(2)}, u32[]{:S(2)}) collective-permute-start(f32[8,384]{1,0:T(8,128)S(1)} %squeeze.98), channel_id=1, source_target_pairs={{0,32},{4,36},{8,40},{12,44},{16,48},{20,52},{24,56},{28,60},{32,6... | collective-permute-start | bytes 36872 | tf_op jit(solution)/shard_map/ppermute | solution.py:22
  (6 other events, 10.4 us)
where the time goes:
time: 262 us; the launch traced here: 258 us
  matrix products  101 us (39%)
  blocking collectives  77.8 us (30%)
  local copies, waits for them, and re-layouts  35.8 us (14%)
  starting transfers between devices  34.2 us (13%)
  other arithmetic  7.85 us (3%)
    dot_general x48, matrix products, one_step(): jnp.dot(right_side.astype(jnp.bfloat16), weights, preferred_element_type=...  91 us
    psum x4, blocking collectives, sum_over_sub(): value = lax.psum(value, axis)  65.6 us
    ppermute x8, starting transfers between devices, passed_along(): return lax.ppermute(value, axis, pairs)  34.2 us
    mul x48, local copies, waits for them, and re-layouts, one_step(): current_now[:, None] * fault_table  16.5 us
    psum x1, blocking collectives, body(): control_local = control_local + lax.psum(control_term, 'scen')  12.1 us
  transfers between devices with their start and end apart: 8, of which 0 were waited for; matrix products, arithmetic and copies ran while one was open for 4% of the time, Pallas kernels for 0%

commit v1 on v0

--- a/solution.py
+++ b/solution.py
@@ -12,7 +12,7 @@
 
 def sum_over_sub(value):
     for axis in reversed(SUB):
-        value = lax.psum(value, axis)
+        value = jnp.sum(lax.all_gather(value, axis), axis=0)
     return value
 
 

time: 262 us -> 271 us (1.034)
  local copies, waits for them, and re-layouts: 35.8 us -> 42.1 us
    psum x4 -> x0, blocking collectives: 65.6 us -> none  [sum_over_sub(): value = lax.psum(value, axis)]
    unnamed x0 -> x4, blocking collectives: none -> 65.1 us
    unnamed x64 -> x73, local copies, waits for them, and re-layouts: 2.87 us -> 8.84 us
  transfers between devices with their start and end apart: 8 -> 8, of which waited for: 0 -> 0; matrix products, arithmetic and copies ran while one was open for 4% -> 6% of each run, Pallas kernels for 0% -> 0%
where the time goes in v1:
time: 271 us; the launch traced here: 267 us
  matrix products  101 us (37%)
  blocking collectives  77.2 us (28%)
  local copies, waits for them, and re-layouts  42.1 us (16%)
  starting transfers between devices  34.2 us (13%)
  other arithmetic  8.51 us (3%)
  between operations  3.96 us (1%)
    dot_general x48, matrix products, one_step(): jnp.dot(right_side.astype(jnp.bfloat16), weights, preferred_element_type=...  91 us
    unnamed x4, blocking collectives  65.1 us
    ppermute x8, starting transfers between devices, passed_along(): return lax.ppermute(value, axis, pairs)  34.2 us
    mul x48, local copies, waits for them, and re-layouts, one_step(): current_now[:, None] * fault_table  16.5 us
    psum x1, blocking collectives, body(): control_local = control_local + lax.psum(control_term, 'scen')  12.1 us
    unnamed x73, local copies, waits for them, and re-layouts  8.84 us
  transfers between devices with their start and end apart: 8, of which 0 were waited for; matrix products, arithmetic and copies ran while one was open for 6% of the time, Pallas kernels for 0%

profile of v1, /device:TPU:4, one launch (start us, length us, event | category | flops | bytes accessed | tf_op | source)
XLA Modules:
  0.0 267.3 jit_solution(66789912903651155)
XLA Ops:
  6.0 2.4 slice_bitcast_fusion
  9.3 2.0 fusion.45
  12.6 45.9 %while.34 = (s32[]{:T(128)}, f32[16,1024]{1,0:T(8,128)S(1)}, f32[24,16,1024]{2,1,0:T(8,128)}, bf16[24,16,1024]{2,1,0:T(8,128)(2,1)}, f32[1,1024]{1,0:T(1,128)S(1...) while((s32[]{:T(128)}, f32[16,1024]{1,0:T(8,128)S(1)}, ...), condition=%wide.region_1.2_spmd.clone, body=%wide.region_0.1_spmd.clone.sunk | while | flops 33685504 | bytes 2528637 | solution.py:103
  14.6 1.9 bitcast_dynamic-update-slice_fusion.4
  18.4 1.9 bitcast_dynamic-update-slice_fusion.4
  24.1 1.9 bitcast_dynamic-update-slice_fusion.4
  35.6 1.9 bitcast_dynamic-update-slice_fusion.4
  39.4 1.9 bitcast_dynamic-update-slice_fusion.4
  45.2 1.9 bitcast_dynamic-update-slice_fusion.4
  47.1 1.9 bitcast_dynamic-update-slice_fusion.4
  49.0 1.9 bitcast_dynamic-update-slice_fusion.4
  52.8 1.9 bitcast_dynamic-update-slice_fusion.4
  54.7 1.9 bitcast_dynamic-update-slice_fusion.4
  58.7 2.3 fusion.57
  63.3 4.8 %collective-permute-start = (f32[8,384]{1,0:T(8,128)}, f32[8,384]{1,0:T(8,128)S(1)}, u32[]{:S(2)}, u32[]{:S(2)}) collective-permute-start(f32[8,384]{1,0:T(8,128)} %squeeze.91), channel_id=1, source_target_pairs={{0,508},{4,0},{8,4},{12,8},{16,12},{20,16},{24,20},{28,24},{32,28}... | collective-permute-start | bytes 36872 | tf_op jit(solution)/shard_map/ppermute | solution.py:22
  68.2 1.9 collective-permute-start.1
  70.8 5.3 %collective-permute-start.2 = (f32[8,384]{1,0:T(8,128)}, f32[8,384]{1,0:T(8,128)}, u32[]{:S(2)}, u32[]{:S(2)}) collective-permute-start(f32[8,384]{1,0:T(8,128)} %squeeze.93), channel_id=1, source_target_pairs={{0,480},{4,484},{8,488},{12,492},{16,496},{20,500},{24,504},{28,50... | collective-permute-start | bytes 36872 | tf_op jit(solution)/shard_map/ppermute | solution.py:22
  76.2 4.4 %collective-permute-start.3 = (f32[8,384]{1,0:T(8,128)S(1)}, f32[8,384]{1,0:T(8,128)}, u32[]{:S(2)}, u32[]{:S(2)}) collective-permute-start(f32[8,384]{1,0:T(8,128)S(1)} %squeeze.94), channel_id=1, source_target_pairs={{0,32},{4,36},{8,40},{12,44},{16,48},{20,52},{24,56},{28,60},{32,6... | collective-permute-start | bytes 36872 | tf_op jit(solution)/shard_map/ppermute | solution.py:22
  98.6 2.0 fusion.43
  101.9 62.0 %while.35 = (s32[]{:T(128)}, f32[16,1024]{1,0:T(8,128)S(1)}, f32[24,16,1024]{2,1,0:T(8,128)}, bf16[24,16,1024]{2,1,0:T(8,128)(2,1)S(1)}, f32[1,1024]{1,0:T(1,128...) while((s32[]{:T(128)}, f32[16,1024]{1,0:T(8,128)S(1)}, ...), condition=%wide.region_3.4_spmd.clone, body=%wide.region_2.3_spmd.clone.sunk | while | flops 33685504 | bytes 2529533 | solution.py:103
  125.8 1.9 bitcast_dynamic-update-slice_fusion.5
  141.4 1.9 bitcast_dynamic-update-slice_fusion.5
  163.9 2.3 multiply_reduce_fusion
  167.7 6.1 %collective-permute-start.4 = (f32[8,384]{1,0:T(8,128)S(1)}, f32[8,384]{1,0:T(8,128)S(1)}, u32[]{:S(2)}, u32[]{:S(2)}) collective-permute-start(f32[8,384]{1,0:T(8,128)S(1)} %squeeze.95), channel_id=1, source_target_pairs={{0,508},{4,0},{8,4},{12,8},{16,12},{20,16},{24,20},{28,24},{32,28}... | collective-permute-start | bytes 36872 | tf_op jit(solution)/shard_map/ppermute | solution.py:22
  173.9 1.9 collective-permute-start.5
  175.9 3.0 %collective-permute-start.6 = (f32[8,384]{1,0:T(8,128)S(1)}, f32[8,384]{1,0:T(8,128)S(1)}, u32[]{:S(2)}, u32[]{:S(2)}) collective-permute-start(f32[8,384]{1,0:T(8,128)S(1)} %squeeze.97), channel_id=1, source_target_pairs={{0,480},{4,484},{8,488},{12,492},{16,496},{20,500},{24,504},{28,50... | collective-permute-start | bytes 36872 | tf_op jit(solution)/shard_map/ppermute | solution.py:22
  179.0 6.7 %collective-permute-start.7 = (f32[8,384]{1,0:T(8,128)S(1)}, f32[8,384]{1,0:T(8,128)S(1)}, u32[]{:S(2)}, u32[]{:S(2)}) collective-permute-start(f32[8,384]{1,0:T(8,128)S(1)} %squeeze.98), channel_id=1, source_target_pairs={{0,32},{4,36},{8,40},{12,44},{16,48},{20,52},{24,56},{28,60},{32,6... | collective-permute-start | bytes 36872 | tf_op jit(solution)/shard_map/ppermute | solution.py:22
  186.8 2.5 all-reduce
  189.6 18.4 %all-reduce.1 = f32[128]{0:T(128)S(1)} all-reduce(f32[128]{0:T(128)S(1)} %dynamic-update-slice.1), channel_id=3, replica_groups=mesh['z_hi'=2,'x'=4,'y'=8,'core'=2,'scen'=4] {'y'}, use_global_device_ids=true, to_apply=%add.1 | all-reduce | flops 128 | bytes 1024
  208.3 32.4 %all-reduce.2 = f32[64]{0:T(128)S(1)} all-reduce(f32[64]{0:T(128)S(1)} %dynamic-update-slice.2), channel_id=4, replica_groups=mesh['z_hi'=2,'x'=4,'y'=8,'core'=2,'scen'=4] {'x'}, use_global_device_ids=true, to_apply=%add.2 | all-reduce | flops 64 | bytes 512
  241.1 11.9 %all-reduce.3 = f32[32]{0:T(128)S(1)} all-reduce(f32[32]{0:T(128)S(1)} %dynamic-update-slice.3), channel_id=5, replica_groups=mesh['z_hi'=2,'x'=4,'y'=8,'core'=2,'scen'=4] {'z_hi'}, use_global_device_ids=true, to_apply=%add.3 | all-reduce | flops 32 | bytes 256
  253.6 12.1 %psum.16 = f32[16]{0:T(128)} all-reduce(f32[16]{0:T(128)S(1)} %add.153), channel_id=1, replica_groups=mesh['z_hi'=2,'x'=4,'y'=8,'core'=2,'scen'=4] {'scen'}, use_global_device_ids=true, to_apply=%region_5.6 | all-reduce | flops 16 | bytes 128 | tf_op jit(solution)/shard_map/psum | solution.py:133
  (284 shorter events, 118.0 us)
Async XLA Ops:
  3.6 5.7 %copy-start.24 = (s32[32]{0:T(128)}, s32[32]{0:T(128)S(1)}, u32[]{:S(2)}) copy-start(s32[32]{0:T(128)S(1)} %eq.71) | copy-start | bytes 388
  5.9 2.5 copy-start.20
  6.0 3.2 %copy-start.29 = (s32[16]{0:T(128)S(1)}, s32[16]{0:T(128)}, u32[]{:S(2)}) copy-start(s32[16]{0:T(128)} %param.29) | copy-start | bytes 196
  9.2 49.5 %copy-start.11 = (pred[1024,32]{0,1:T(8,128)(4,1)}, pred[1024,32]{0,1:T(8,128)(4,1)S(1)}, u32[]{:S(2)}) copy-start(pred[1024,32]{0,1:T(8,128)(4,1)S(1)} %iota_compare_fusion.5) | copy-start | bytes 98308
  9.2 3.4 %copy-start.26 = (f32[32]{0:T(128)}, f32[32]{0:T(128)S(1)}, u32[]{:S(2)}) copy-start(f32[32]{0:T(128)S(1)} %broadcast_select_fusion) | copy-start | bytes 388
  9.2 3.4 %copy-start = (bf16[1,1024,1024]{2,1,0:T(8,128)(2,1)S(1)}, bf16[1,1024,1024]{2,1,0:T(8,128)(2,1)}, u32[]{:S(2)}) copy-start(bf16[1,1024,1024]{2,1,0:T(8,128)(2,1)} %param.18) | copy-start | bytes 6291460
  9.3 3.4 %copy-start.3 = (f32[1,16,1024]{2,1,0:T(8,128)S(1)}, f32[1,16,1024]{2,1,0:T(8,128)}, u32[]{:S(2)}) copy-start(f32[1,16,1024]{2,1,0:T(8,128)} %param.20) | copy-start | bytes 196612
  9.3 3.3 %copy-start.9 = (f32[1,1024]{1,0:T(1,128)S(1)}, f32[1,1024]{1,0:T(1,128)}, u32[]{:S(2)}) copy-start(f32[1,1024]{1,0:T(1,128)} %param.21) | copy-start | bytes 12292
  12.6 45.9 %copy-start.28 = (s32[1,16]{1,0:T(1,128)S(1)}, s32[1,16]{1,0:T(1,128)}, u32[]{:S(2)}) copy-start(s32[1,16]{1,0:T(1,128)} %param.27) | copy-start | bytes 196
  61.6 19.8 %copy-start.8 = (f32[1,48,16,16]{1,3,2,0:T(8,128)S(1)}, f32[1,48,16,16]{1,3,2,0:T(8,128)}, u32[]{:S(2)}) copy-start(f32[1,48,16,16]{1,3,2,0:T(8,128)} %param.28) | copy-start | bytes 147460
  61.6 20.4 %copy-start.21 = (f32[48,16]{0,1:T(8,128)S(1)}, f32[48,16]{0,1:T(8,128)}, u32[]{:S(2)}) copy-start(f32[48,16]{0,1:T(8,128)} %param.31) | copy-start | bytes 9220
  61.8 20.3 %copy-start.22 = (f32[24,16]{0,1:T(8,128)S(1)}, f32[24,16]{0,1:T(8,128)}, u32[]{:S(2)}) copy-start(f32[24,16]{0,1:T(8,128)} %get-tuple-element.466) | copy-start | bytes 4612
  63.3 31.3 %collective-permute-start = (f32[8,384]{1,0:T(8,128)}, f32[8,384]{1,0:T(8,128)S(1)}, u32[]{:S(2)}, u32[]{:S(2)}) collective-permute-start(f32[8,384]{1,0:T(8,128)} %squeeze.91), channel_id=1, source_target_pairs={{0,508},{4,0},{8,4},{12,8},{16,12},{20,16},{24,20},{28,24},{32,28}... | collective-permute-start | bytes 36872 | tf_op jit(solution)/shard_map/ppermute | solution.py:22
  68.2 26.6 %collective-permute-start.1 = (f32[8,384]{1,0:T(8,128)S(1)}, f32[8,384]{1,0:T(8,128)S(1)}, u32[]{:S(2)}, u32[]{:S(2)}) collective-permute-start(f32[8,384]{1,0:T(8,128)S(1)} %squeeze.92), channel_id=1, source_target_pairs={{0,4},{4,8},{8,12},{12,16},{16,20},{20,24},{24,28},{28,32},{32,36}... | collective-permute-start | bytes 36872 | tf_op jit(solution)/shard_map/ppermute | solution.py:22
  70.8 24.2 %collective-permute-start.2 = (f32[8,384]{1,0:T(8,128)}, f32[8,384]{1,0:T(8,128)}, u32[]{:S(2)}, u32[]{:S(2)}) collective-permute-start(f32[8,384]{1,0:T(8,128)} %squeeze.93), channel_id=1, source_target_pairs={{0,480},{4,484},{8,488},{12,492},{16,496},{20,500},{24,504},{28,50... | collective-permute-start | bytes 36872 | tf_op jit(solution)/shard_map/ppermute | solution.py:22
  76.2 19.7 %collective-permute-start.3 = (f32[8,384]{1,0:T(8,128)S(1)}, f32[8,384]{1,0:T(8,128)}, u32[]{:S(2)}, u32[]{:S(2)}) collective-permute-start(f32[8,384]{1,0:T(8,128)S(1)} %squeeze.94), channel_id=1, source_target_pairs={{0,32},{4,36},{8,40},{12,44},{16,48},{20,52},{24,56},{28,60},{32,6... | collective-permute-start | bytes 36872 | tf_op jit(solution)/shard_map/ppermute | solution.py:22
  93.0 5.5 %copy-start.25 = (s32[32]{0:T(128)S(1)}, s32[32]{0:T(128)}, u32[]{:S(2)}) copy-start(s32[32]{0:T(128)} %copy-done.24) | copy-start | bytes 388
  93.0 5.5 %copy-start.27 = (f32[32]{0:T(128)S(1)}, f32[32]{0:T(128)}, u32[]{:S(2)}) copy-start(f32[32]{0:T(128)} %copy-done.26) | copy-start | bytes 388
  95.9 2.5 copy-start.4
  101.9 62.0 %copy-start.13 = (f32[16,1024]{1,0:T(8,128)S(1)}, f32[16,1024]{1,0:T(8,128)}, u32[]{:S(2)}) copy-start(f32[16,1024]{1,0:T(8,128)} %fusion.55) | copy-start | bytes 196612
  163.9 2.4 copy-start.1
  163.9 2.4 copy-start.12
  167.2 18.6 %copy-start.18 = (f32[24,16]{1,0:T(8,128)S(1)}, f32[24,16]{1,0:T(8,128)}, u32[]{:S(2)}) copy-start(f32[24,16]{1,0:T(8,128)} %copy.62) | copy-start | bytes 4612
  167.2 18.6 %copy-start.19 = (f32[24,16]{1,0:T(8,128)S(1)}, f32[24,16]{1,0:T(8,128)}, u32[]{:S(2)}) copy-start(f32[24,16]{1,0:T(8,128)} %copy.63) | copy-start | bytes 4612
  167.2 18.7 %copy-start.16 = (f32[384,16]{0,1:T(8,128)S(1)}, f32[384,16]{0,1:T(8,128)}, u32[]{:S(2)}) copy-start(f32[384,16]{0,1:T(8,128)} %squeeze.100) | copy-start | bytes 73732
  167.2 18.7 %copy-start.17 = (f32[384,16]{0,1:T(8,128)S(1)}, f32[384,16]{0,1:T(8,128)}, u32[]{:S(2)}) copy-start(f32[384,16]{0,1:T(8,128)} %squeeze.99) | copy-start | bytes 73732
  167.4 99.0 %copy-start.5 = (f32[1,8,24,16]{2,3,1,0:T(8,128)S(1)}, f32[1,8,24,16]{2,3,1,0:T(8,128)}, u32[]{:S(2)}) copy-start(f32[1,8,24,16]{2,3,1,0:T(8,128)} %copy-done.4) | copy-start | bytes 36868
  167.4 99.0 %copy-start.7 = (f32[1,8,24,16]{2,3,1,0:T(8,128)S(1)}, f32[1,8,24,16]{2,3,1,0:T(8,128)}, u32[]{:S(2)}) copy-start(f32[1,8,24,16]{2,3,1,0:T(8,128)} %copy-done.6) | copy-start | bytes 36868
  167.7 98.0 %collective-permute-start.4 = (f32[8,384]{1,0:T(8,128)S(1)}, f32[8,384]{1,0:T(8,128)S(1)}, u32[]{:S(2)}, u32[]{:S(2)}) collective-permute-start(f32[8,384]{1,0:T(8,128)S(1)} %squeeze.95), channel_id=1, source_target_pairs={{0,508},{4,0},{8,4},{12,8},{16,12},{20,16},{24,20},{28,24},{32,28}... | collective-permute-start | bytes 36872 | tf_op jit(solution)/shard_map/ppermute | solution.py:22
  173.9 92.0 %collective-permute-start.5 = (f32[8,384]{1,0:T(8,128)S(1)}, f32[8,384]{1,0:T(8,128)S(1)}, u32[]{:S(2)}, u32[]{:S(2)}) collective-permute-start(f32[8,384]{1,0:T(8,128)S(1)} %squeeze.96), channel_id=1, source_target_pairs={{0,4},{4,8},{8,12},{12,16},{16,20},{20,24},{24,28},{28,32},{32,36}... | collective-permute-start | bytes 36872 | tf_op jit(solution)/shard_map/ppermute | solution.py:22
  175.9 90.2 %collective-permute-start.6 = (f32[8,384]{1,0:T(8,128)S(1)}, f32[8,384]{1,0:T(8,128)S(1)}, u32[]{:S(2)}, u32[]{:S(2)}) collective-permute-start(f32[8,384]{1,0:T(8,128)S(1)} %squeeze.97), channel_id=1, source_target_pairs={{0,480},{4,484},{8,488},{12,492},{16,496},{20,500},{24,504},{28,50... | collective-permute-start | bytes 36872 | tf_op jit(solution)/shard_map/ppermute | solution.py:22
  179.0 87.2 %collective-permute-start.7 = (f32[8,384]{1,0:T(8,128)S(1)}, f32[8,384]{1,0:T(8,128)S(1)}, u32[]{:S(2)}, u32[]{:S(2)}) collective-permute-start(f32[8,384]{1,0:T(8,128)S(1)} %squeeze.98), channel_id=1, source_target_pairs={{0,32},{4,36},{8,40},{12,44},{16,48},{20,52},{24,56},{28,60},{32,6... | collective-permute-start | bytes 36872 | tf_op jit(solution)/shard_map/ppermute | solution.py:22
  (6 other events, 10.4 us)
